TPU v7x, 512 devices: a whole 4x4x16 slice. The times are simulated.
512 devices in a mesh: tok: 64 (over z, x), head: 8 (over y, core).
Axes of the slice: x: 4, y: 4, z: 16, core: 2. Of those that a mesh axis runs over, the one named last changes fastest.
Arguments:
- tokens: bfloat16 [32768, 2560], P('tok', 'head'), may hold values from -6 to 6
- query_weight: bfloat16 [2560, 2560], P('tok'), may hold values from -0.125 to 0.125
- keyvalue_weight: bfloat16 [2560, 512], P('tok'), may hold values from -0.125 to 0.125
- output_weight: bfloat16 [2560, 2560], P(None, ('head', 'tok')), may hold values from -0.125 to 0.125
- cache: bfloat16 [2048, 2, 128, 256], P(('tok', 'head')), may hold values from -460 to 460
- page_table: int32 [512, 4], P('tok'), may hold values from 0 to 2047, as said below
- parents: int32 [512, 64], P('tok'), may hold values from 0 to 62, as said below
- cache_len: int32 [512], P('tok'), may hold values from 1 to 448, as said below
- accepted_leaf: int32 [512], P('tok'), may hold values from 0 to 63
Outputs:
- attended: bfloat16 [32768, 2560], P('tok', 'head')
- cache_out: bfloat16 [2048, 2, 128, 256], P(('tok', 'head'))
Inputs may be any that keep to these rules, and one draw needn't show every extreme that they name: `page_table`: for every d, row d names each of the pages d * 4 to d * 4 + 3 exactly once, so request d's pages all lie on device d (devices counted tok-major, head-minor). parents[r, 0] = 0, and parents[r, i] < i for i >= 1. `cache_len`: roughly half of the requests hold at most 128 cached positions, the others more than 320.
All inputs are finite; a program needn't handle non-finite values.
Results may differ from a plain program's by a relative error of at most 0.014.
The roundings to bfloat16 on the way count: a program that leaves them out, or rounds other values in their place, can miss the bound.
Values may be sent and summed in bfloat16 or wider, within the bound.
No kernel may reach another device: no remote copies, remote signals or barrier semaphores. Data moves between devices by JAX's collectives and lax.ppermute only.
A program may use at most 64 MiB of HBM per device.

v0:
```python
import math

import jax
import jax.numpy as jnp
from jax import lax
from jax.sharding import PartitionSpec as P

HQ = 10
HD = 256
DRAFT = 64
PAGE = 128
NPR = 4
WINDOW = 256


def ancestry(parent_row):
    node_ids = jnp.arange(DRAFT, dtype=jnp.int32)
    link = (parent_row[:, None] == node_ids[None, :]).astype(jnp.float32)
    reach = jnp.minimum(link + jnp.eye(DRAFT, dtype=jnp.float32), 1.0)
    for sweep in range((DRAFT - 1).bit_length()):
        reach = jnp.minimum(jnp.dot(reach, reach, precision=lax.Precision.HIGHEST), 1.0)
    depth = (jnp.sum(reach, axis=1) - 1.0).astype(jnp.int32)
    return (reach, depth)


def rotate(values, position):
    half = HD // 4
    freq = jnp.exp(jnp.arange(half, dtype=jnp.float32) * (-2.0 * math.log(10000.0) / (HD // 2)))
    angle = position.astype(jnp.float32)[..., None] * freq
    cosine = jnp.cos(angle)
    sine = jnp.sin(angle)
    first = values[..., :half]
    second = values[..., half : 2 * half]
    return jnp.concatenate(
        [first * cosine - second * sine, second * cosine + first * sine, values[..., 2 * half :]],
        axis=-1,
    )


def attend(queries, cache_keys, cache_values, tree_keys, tree_values, lengths, position, reach):
    window_span = cache_keys.shape[1]
    slot_ids = jnp.arange(window_span, dtype=jnp.int32)
    visible = (slot_ids[None, None, :] < lengths[:, None, None]) & (
        slot_ids[None, None, :] > position[:, :, None] - WINDOW
    )
    cache_scores = jnp.einsum(
        "rnhd,rcd->rhnc", queries, cache_keys, preferred_element_type=jnp.float32
    )
    tree_scores = jnp.einsum(
        "rnhd,rmd->rhnm", queries, tree_keys, preferred_element_type=jnp.float32
    )
    cache_scores = jnp.where(visible[:, None], cache_scores, -1e30)
    tree_scores = jnp.where(reach[:, None] > 0.5, tree_scores, -1e30)
    row_peak = jnp.maximum(jnp.max(cache_scores, axis=-1), jnp.max(tree_scores, axis=-1))[..., None]
    cache_weights = jnp.exp(cache_scores - row_peak)
    tree_weights = jnp.exp(tree_scores - row_peak)
    denominator = jnp.sum(cache_weights, axis=-1, keepdims=True) + jnp.sum(
        tree_weights, axis=-1, keepdims=True
    )
    cache_weights = (cache_weights / denominator).astype(jnp.bfloat16)
    tree_weights = (tree_weights / denominator).astype(jnp.bfloat16)
    result = jnp.einsum(
        "rhnc,rcd->rnhd", cache_weights, cache_values, preferred_element_type=jnp.float32
    )
    result = result + jnp.einsum(
        "rhnm,rmd->rnhd", tree_weights, tree_values, preferred_element_type=jnp.float32
    )
    return result.astype(jnp.bfloat16)


def refresh(logical_pages, length, leaf, reach, depth, new_keys, new_values):
    count = logical_pages.shape[0] * logical_pages.shape[2]
    logical = jnp.transpose(logical_pages, (1, 0, 2, 3)).reshape(2, count, HD)
    slot_ids = jnp.arange(count, dtype=jnp.int32)
    on_path = reach[leaf]
    selector = ((on_path[None, :] > 0.5) & (depth[None, :] == slot_ids[:, None] - length)).astype(
        jnp.float32
    )
    placed_keys = jnp.dot(selector, new_keys.astype(jnp.float32), precision=lax.Precision.HIGHEST)
    placed_values = jnp.dot(
        selector, new_values.astype(jnp.float32), precision=lax.Precision.HIGHEST
    )
    placed = jnp.stack([placed_keys, placed_values]).astype(jnp.bfloat16)
    written = jnp.sum(selector, axis=1) > 0.5
    logical = jnp.where(written[None, :, None], placed, logical)
    return jnp.transpose(
        logical.reshape(2, logical_pages.shape[0], logical_pages.shape[2], HD), (1, 0, 2, 3)
    )


def contract(source, piece):
    return jnp.dot(source, piece, preferred_element_type=jnp.float32)


def project_memory(rows, keyvalue_weight, position):
    projected = contract(rows, lax.all_gather(keyvalue_weight, "tok", axis=0, tiled=True))
    new_keys = rotate(projected[:, :HD], position).astype(jnp.bfloat16)
    new_values = projected[:, HD:].astype(jnp.bfloat16)
    return (new_keys, new_values)


def split_pages(page_blocks, count):
    cache_keys = page_blocks[:, :, 0].reshape(count, NPR * PAGE, HD)
    cache_values = page_blocks[:, :, 1].reshape(count, NPR * PAGE, HD)
    return (cache_keys, cache_values)


def reduce_heads(mixed, output_weight, safe_heads, head_mask, slots_per):
    head_count = lax.axis_size("head")
    tok_count = lax.axis_size("tok")
    narrow = output_weight.shape[1]
    blocks = lax.all_gather(output_weight, "head", axis=1, tiled=True)
    part_cols = blocks.shape[1]
    my_output_weight = (
        jnp.take(blocks.reshape(HQ, HD, part_cols), safe_heads, axis=0) * head_mask[:, None, None]
    )
    my_output_weight = my_output_weight.reshape(slots_per * HD, part_cols)
    partial_value = jnp.dot(
        mixed,
        lax.all_gather(my_output_weight, "tok", axis=1, tiled=True),
        preferred_element_type=jnp.float32,
    ).astype(jnp.bfloat16)
    row_count = partial_value.shape[0]
    partial_value = partial_value.reshape(row_count, tok_count, head_count, narrow)
    partial_value = jnp.transpose(partial_value, (0, 2, 1, 3)).reshape(
        row_count, tok_count * head_count * narrow
    )
    partial_value = lax.optimization_barrier(partial_value)
    summed = lax.psum_scatter(
        partial_value.astype(jnp.float32).astype(jnp.bfloat16),
        "head",
        scatter_dimension=1,
        tiled=True,
    )
    return summed


def shards(
    tokens,
    query_weight,
    keyvalue_weight,
    output_weight,
    cache,
    page_table,
    parents,
    cache_len,
    accepted_leaf,
):
    head_count = lax.axis_size("head")
    head_index = lax.axis_index("head")
    tok_index = lax.axis_index("tok")
    slots_per = -(-HQ // head_count)
    requests = parents.shape[0]
    owned = requests // head_count
    rows_owned = owned * DRAFT
    pages_dev = cache.shape[0]
    gathered = lax.all_gather(tokens, "head", axis=1, tiled=True)
    wide = gathered.astype(jnp.float32)
    mean_square = jnp.mean(wide * wide, axis=1, keepdims=True)
    normed = (wide * lax.rsqrt(mean_square + 1e-06)).astype(jnp.bfloat16)
    reach, depth = jax.vmap(ancestry)(parents)
    position = cache_len[:, None] + depth
    flat_pos = position.reshape(-1)
    head_ids = head_index + head_count * jnp.arange(slots_per, dtype=jnp.int32)
    usable = head_ids < HQ
    safe_heads = jnp.minimum(head_ids, HQ - 1)
    head_mask = usable.astype(jnp.bfloat16)
    part_rows = query_weight.shape[0]
    my_query_weight = (
        jnp.take(query_weight.reshape(part_rows, HQ, HD), safe_heads, axis=1)
        * head_mask[None, :, None]
    )
    my_query_weight = my_query_weight.reshape(part_rows, slots_per * HD)
    queries = contract(normed, lax.all_gather(my_query_weight, "tok", axis=0, tiled=True))
    queries = (rotate(queries.reshape(-1, slots_per, HD), flat_pos[:, None]) * HD ** (-0.5)).astype(
        jnp.bfloat16
    )
    own_start = head_index * rows_owned
    own_reach = lax.dynamic_slice_in_dim(reach, head_index * owned, owned, 0)
    own_depth = lax.dynamic_slice_in_dim(depth, head_index * owned, owned, 0)
    own_len = lax.dynamic_slice_in_dim(cache_len, head_index * owned, owned, 0)
    own_leaf = lax.dynamic_slice_in_dim(accepted_leaf, head_index * owned, owned, 0)
    device = tok_index * head_count + head_index
    own_table = (
        lax.dynamic_slice_in_dim(page_table, head_index * owned, owned, 0) - device * pages_dev
    )
    own_pages = jnp.take(cache, own_table.reshape(-1), axis=0).reshape(owned, NPR, 2, PAGE, HD)
    tree_keys, tree_values = project_memory(normed, keyvalue_weight, flat_pos)
    own_keys = lax.dynamic_slice_in_dim(tree_keys, own_start, rows_owned, 0)
    own_values = lax.dynamic_slice_in_dim(tree_values, own_start, rows_owned, 0)
    page_pool = lax.all_gather(cache, "head", axis=0, tiled=True)
    local_ids = page_table - tok_index * head_count * pages_dev
    page_blocks = jnp.take(page_pool, local_ids.reshape(-1), axis=0).reshape(
        requests, NPR, 2, PAGE, HD
    )
    cache_keys, cache_values = split_pages(page_blocks, requests)
    result = attend(
        queries.reshape(requests, DRAFT, slots_per, HD),
        cache_keys,
        cache_values,
        tree_keys.reshape(requests, DRAFT, HD),
        tree_values.reshape(requests, DRAFT, HD),
        cache_len,
        position,
        reach,
    )
    mixed = result.reshape(-1, slots_per * HD)
    attended = reduce_heads(mixed, output_weight, safe_heads, head_mask, slots_per)
    new_pages = jax.vmap(refresh)(
        own_pages,
        own_len,
        own_leaf,
        own_reach,
        own_depth,
        own_keys.reshape(owned, DRAFT, HD),
        own_values.reshape(owned, DRAFT, HD),
    )
    flat_ids = own_table.reshape(-1)
    matches = (flat_ids[:, None] == jnp.arange(pages_dev, dtype=jnp.int32)[None, :]).astype(
        jnp.int32
    )
    inverse = jnp.sum(matches * jnp.arange(pages_dev, dtype=jnp.int32)[:, None], axis=0)
    cache_out = jnp.take(new_pages.reshape(pages_dev, 2, PAGE, HD), inverse, axis=0)
    return (attended, cache_out)


def solution(mesh):
    in_specs = (
        P("tok", "head"),
        P("tok", None),
        P("tok", None),
        P(None, ("head", "tok")),
        P(("tok", "head"), None, None, None),
        P("tok", None),
        P("tok", None),
        P("tok"),
        P("tok"),
    )
    out_specs = (P("tok", "head"), P(("tok", "head"), None, None, None))
    return jax.shard_map(shards, mesh=mesh, in_specs=in_specs, out_specs=out_specs, check_vma=False)
```

profile of v0, /device:TPU:1, one launch (start us, length us, event | category | flops | bytes accessed | tf_op | source)
XLA Modules:
  0.0 581.3 jit_solution(10205464197976937876)
XLA Ops:
  7.2 0.7 all-gather.9.cloned.1.call-update
  8.0 0.7 all-gather.13.cloned.1.call-update
  8.9 0.9 copy.116
  9.9 0.6 gather_fusion.1
  10.4 0.6 select_multiply_fusion.1
  11.1 0.5 all-gather.7.cloned.1.call-update
  11.7 19.8 %all-gather = bf16[8,5,2560]{2,1,0:T(8,128)(2,1)S(1)} all-gather(bf16[1,5,2560]{2,1,0:T(8,128)(2,1)} %bitcast.138), channel_id=1, replica_groups=mesh['tok'=64,'head'=8] {'head'}, dimensions={0}, use_global_device_ids=true | all-gather | bytes 230400 | tf_op jit(solution)/shard_map/all_gather | solution.py:112
  31.7 0.6 gather_fusion.2
  32.2 0.6 select_multiply_fusion
  33.0 0.5 convolution_minimum_fusion.5
  33.5 0.4 convolution_minimum_fusion.4
  33.9 0.4 convolution_minimum_fusion.3
  34.3 0.4 convolution_minimum_fusion.2
  34.7 0.4 convolution_minimum_fusion.1
  35.1 0.5 fusion.58
  35.8 0.8 copy.86
  36.7 0.6 copy.75
  37.4 0.3 fusion.16
  37.7 11.9 %all-gather.9.cloned.1.call-done = bf16[512,2560]{0,1:T(8,128)(2,1)} async-done(((bf16[512,320]{0,1:T(8,128)(2,1)}), bf16[512,2560]{0,1:T(8,128)(2,1)}) %all-gather.9.cloned.1.call-update) | async-done | bytes 2621456 | tf_op jit(solution)/shard_map/all_gather | solution.py:157
  49.6 2.5 fusion
  52.1 133.4 %all-gather.13.cloned.1.call-done = bf16[2560,512]{1,0:T(8,128)(2,1)} async-done(((bf16[40,512]{1,0:T(8,128)(2,1)}), bf16[2560,512]{1,0:T(8,128)(2,1)}) %all-gather.13.cloned.1.call-update) | async-done | bytes 2621456 | tf_op jit(solution)/shard_map/all_gather | solution.py:96
  185.5 3.3 fusion.2
  188.8 0.7 slice.107
  189.5 0.7 slice.106
  190.3 1.9 multiply_cosine_fusion
  192.2 1.1 copy.80
  193.2 0.8 copy.81
  194.0 131.7 %all-gather.11.cloned.1.call-done = bf16[2560,512]{1,0:T(8,128)(2,1)} async-done(((bf16[40,512]{1,0:T(8,128)(2,1)}), bf16[2560,512]{1,0:T(8,128)(2,1)}) %all-gather.11.cloned.1.call-update) | async-done | bytes 2621456 | tf_op jit(solution)/shard_map/all_gather | solution.py:174
  325.7 3.3 fusion.4
  329.2 0.1 concatenate.41
  329.4 0.2 copy.83
  329.6 0.1 concatenate.42
  329.7 0.2 copy.84
  330.0 0.2 copy.99
  330.2 0.6 fusion.59
  330.8 41.5 %all-gather.7.cloned.1.call-done = bf16[32,2,128,256]{3,2,1,0:T(8,128)(2,1)} async-done(((bf16[4,2,128,256]{3,2,1,0:T(8,128)(2,1)}), bf16[32,2,128,256]{3,2,1,0:T(8,128)(2,1)}) %all-gather.7.cloned.1.call-update) | async-done | bytes 4194320 | tf_op jit(solution)/shard_map/all_gather | solution.py:191
  372.3 5.1 gather_fusion
  377.4 2.7 copy_select_fusion
  380.0 0.5 fusion.56
  380.5 1.0 fusion.6
  381.5 0.1 fusion.18
  381.7 0.7 fusion.7
  382.4 0.1 copy-done.6
  382.5 0.4 fusion.19
  382.8 0.9 fusion.9
  383.7 0.5 copy.88
  384.4 123.2 %all-gather.15.cloned.1.call-done = bf16[512,2560]{0,1:T(8,128)(2,1)} async-done(((bf16[512,40]{0,1:T(8,128)(2,1)}), bf16[512,2560]{0,1:T(8,128)(2,1)}) %all-gather.15.cloned.1.call-update) | async-done | bytes 2621456 | tf_op jit(solution)/shard_map/all_gather | solution.py:120
  507.6 4.8 convolution_convert_fusion
  512.4 3.0 copy.91
  515.4 2.9 reshape.548
  518.3 4.6 copy.92
  522.9 6.2 %reshape.549 = bf16[512,2560]{0,1:T(8,128)(2,1)} reshape(bf16[512,8,64,5]{0,3,2,1:T(8,128)(2,1)} %copy.92) | data formatting | bytes 5242880 | tf_op jit(solution)/shard_map/reshape | solution.py:125
  529.1 0.6 dynamic_slice.24
  529.8 0.6 dynamic_slice.22
  531.6 0.2 subtract_reduce_fusion
  531.9 0.6 gather_fusion.3
  532.5 0.1 select_bitcast_fusion
  533.4 0.5 iota_subtract_fusion
  534.1 1.0 fusion.12
  535.1 0.3 fusion.11
  535.4 0.2 maximum_select_fusion
  535.7 0.6 gather_fusion.4
  536.3 0.9 broadcast_select_fusion
  537.2 37.3 %reduce-scatter.2.cloned.1.call-done = bf16[512,320]{0,1:T(8,128)(2,1)} async-done(((bf16[512,2560]{0,1:T(8,128)(2,1)}), bf16[512,320]{0,1:T(8,128)(2,1)}) %reduce-scatter.2.cloned.1.call-update) | async-done | bytes 327696 | tf_op jit(solution)/shard_map/reduce_scatter | solution.py:129
  (78 shorter events, 1.9 us)
Async XLA Ops:
  7.2 25.8 %copy-start.12 = (s32[8,64]{1,0:T(8,128)S(1)}, s32[8,64]{1,0:T(8,128)}, u32[]{:S(2)}) copy-start(s32[8,64]{1,0:T(8,128)} %param.17) | copy-start | bytes 6148
  7.2 42.4 %all-gather.9.cloned.1.call-start = ((), (), s32[]{:S(2)}) async-start(), calls=%async_computation.2 | async-start | bytes 2949120 | tf_op jit(solution)/shard_map/all_gather | solution.py:157
  7.9 177.6 %all-gather.13.cloned.1.call-start = ((), (), s32[]{:S(2)}) async-start(), calls=%async_computation.4 | async-start | bytes 2662400 | tf_op jit(solution)/shard_map/all_gather | solution.py:96
  8.7 317.1 %all-gather.11.cloned.1.call-start = ((), (), s32[]{:S(2)}) async-start(), calls=%async_computation.3 | async-start | bytes 2662400 | tf_op jit(solution)/shard_map/all_gather | solution.py:174
  11.1 361.2 %all-gather.7.cloned.1.call-start = ((), (), s32[]{:S(2)}) async-start(), calls=%async_computation.1 | async-start | bytes 4718592 | tf_op jit(solution)/shard_map/all_gather | solution.py:191
  11.7 495.9 %all-gather.15.cloned.1.call-start = ((), (), s32[]{:S(2)}) async-start(), calls=%async_computation.5 | async-start | bytes 2662400 | tf_op jit(solution)/shard_map/all_gather | solution.py:120
  31.6 3.9 copy-start.9
  31.6 4.9 copy-start.8
  32.9 541.6 %reduce-scatter.2.cloned.1.call-start = ((), (), s32[]{:S(2)}) async-start(), calls=%async_computation.6 | async-start | bytes 2949120 | tf_op jit(solution)/shard_map/reduce_scatter | solution.py:129
  49.6 135.9 %copy-start = (bf16[512,2560]{0,1:T(8,128)(2,1)S(1)}, bf16[512,2560]{0,1:T(8,128)(2,1)}, u32[]{:S(2)}) copy-start(bf16[512,2560]{0,1:T(8,128)(2,1)} %all-gather.9.cloned.1.call-done) | copy-start | bytes 7864324
  52.1 136.7 %copy-start.10 = (f32[512]{0:T(512)}, f32[512]{0:T(512)S(1)}, u32[]{:S(2)}) copy-start(f32[512]{0:T(512)S(1)} %add_rsqrt_fusion) | copy-start | bytes 6148
  194.0 135.1 %copy-start.2 = (f32[512,64]{0,1:T(8,128)S(1)}, f32[512,64]{0,1:T(8,128)}, u32[]{:S(2)}) copy-start(f32[512,64]{0,1:T(8,128)} %copy.81) | copy-start | bytes 393220
  329.2 1.0 copy-start.3
  329.2 1.0 copy-start.4
  329.2 1.0 copy-start.5
  329.2 1.0 copy-start.7
  330.8 46.5 %copy-start.11 = (pred[8,4]{1,0:T(8,128)(4,1)S(1)}, pred[8,4]{1,0:T(8,128)(4,1)}, u32[]{:S(2)}) copy-start(pred[8,4]{1,0:T(8,128)(4,1)} %copy.75) | copy-start | bytes 100
  381.5 1.0 copy-start.6
  529.1 0.7 copy-start.13
  529.1 2.8 copy-start.1
Sparse Core Ops, SparseCore 0:
  10.1 39.4 all-gather.8
  52.5 132.9 all-gather.12
  188.5 137.1 all-gather.10
  327.7 44.5 all-gather.6
  375.1 132.4 all-gather.14
  529.3 45.1 reduce-scatter.1
where the time goes:
time: 583 us; the launch traced here: 581 us
  waiting for transfers between devices  481 us (83%)
  local copies, waits for them, and re-layouts  33.8 us (6%)
  blocking collectives  19.8 us (3%)
  matrix products  18.1 us (3%)
  between operations  16.5 us (3%)
  other arithmetic  12 us (2%)
    all_gather x1, waiting for transfers between devices, project_memory(): lax.all_gather(keyvalue_weight, 'tok', axis=0, tiled=True)  133 us
    all_gather x1, waiting for transfers between devices, shards(): lax.all_gather(my_query_weight, 'tok', axis=0, tiled=True)  132 us
    all_gather x1, waiting for transfers between devices, reduce_heads(): lax.all_gather(my_output_weight, 'tok', axis=1, tiled=True)  123 us
    all_gather x1, waiting for transfers between devices, shards(): page_pool = lax.all_gather(cache, 'head', axis=0, tiled=True)  41.5 us
    reduce_scatter x1, waiting for transfers between devices, reduce_heads(): lax.psum_scatter(partial_value.astype(jnp.float32).astype(jnp.bfloat16),...  37.3 us
    all_gather x1, blocking collectives, reduce_heads(): blocks = lax.all_gather(output_weight, 'head', axis=1, tiled=True)  19.8 us
    all_gather x1, waiting for transfers between devices, shards(): gathered = lax.all_gather(tokens, 'head', axis=1, tiled=True)  11.9 us
  transfers between devices with their start and end apart: 6, of which 6 were waited for; matrix products, arithmetic and copies ran while one was open for 7% of the time, Pallas kernels for 0%

commit v1 on v0

v1 whole, which is shorter than its diff:
```python
import math

import jax
import jax.numpy as jnp
from jax import lax
from jax.sharding import PartitionSpec as P

HQ = 10
HD = 256
DRAFT = 64
PAGE = 128
NPR = 4
WINDOW = 256


def ancestry(parent_row):
    node_ids = jnp.arange(DRAFT, dtype=jnp.int32)
    link = (parent_row[:, None] == node_ids[None, :]).astype(jnp.float32)
    reach = jnp.minimum(link + jnp.eye(DRAFT, dtype=jnp.float32), 1.0)
    for sweep in range((DRAFT - 1).bit_length()):
        reach = jnp.minimum(jnp.dot(reach, reach, precision=lax.Precision.HIGHEST), 1.0)
    depth = (jnp.sum(reach, axis=1) - 1.0).astype(jnp.int32)
    return (reach, depth)


def rotate(values, position):
    half = HD // 4
    freq = jnp.exp(jnp.arange(half, dtype=jnp.float32) * (-2.0 * math.log(10000.0) / (HD // 2)))
    angle = position.astype(jnp.float32)[..., None] * freq
    cosine = jnp.cos(angle)
    sine = jnp.sin(angle)
    first = values[..., :half]
    second = values[..., half : 2 * half]
    return jnp.concatenate(
        [first * cosine - second * sine, second * cosine + first * sine, values[..., 2 * half :]],
        axis=-1,
    )


def attend(queries, cache_keys, cache_values, tree_keys, tree_values, lengths, position, reach):
    window_span = cache_keys.shape[1]
    slot_ids = jnp.arange(window_span, dtype=jnp.int32)
    visible = (slot_ids[None, None, :] < lengths[:, None, None]) & (
        slot_ids[None, None, :] > position[:, :, None] - WINDOW
    )
    cache_scores = jnp.einsum(
        "rnhd,rcd->rhnc", queries, cache_keys, preferred_element_type=jnp.float32
    )
    tree_scores = jnp.einsum(
        "rnhd,rmd->rhnm", queries, tree_keys, preferred_element_type=jnp.float32
    )
    cache_scores = jnp.where(visible[:, None], cache_scores, -1e30)
    tree_scores = jnp.where(reach[:, None] > 0.5, tree_scores, -1e30)
    row_peak = jnp.maximum(jnp.max(cache_scores, axis=-1), jnp.max(tree_scores, axis=-1))[..., None]
    cache_weights = jnp.exp(cache_scores - row_peak)
    tree_weights = jnp.exp(tree_scores - row_peak)
    denominator = jnp.sum(cache_weights, axis=-1, keepdims=True) + jnp.sum(
        tree_weights, axis=-1, keepdims=True
    )
    cache_weights = (cache_weights / denominator).astype(jnp.bfloat16)
    tree_weights = (tree_weights / denominator).astype(jnp.bfloat16)
    result = jnp.einsum(
        "rhnc,rcd->rnhd", cache_weights, cache_values, preferred_element_type=jnp.float32
    )
    result = result + jnp.einsum(
        "rhnm,rmd->rnhd", tree_weights, tree_values, preferred_element_type=jnp.float32
    )
    return result.astype(jnp.bfloat16)


def refresh(logical_pages, length, leaf, reach, depth, new_keys, new_values):
    count = logical_pages.shape[0] * logical_pages.shape[2]
    logical = jnp.transpose(logical_pages, (1, 0, 2, 3)).reshape(2, count, HD)
    slot_ids = jnp.arange(count, dtype=jnp.int32)
    on_path = reach[leaf]
    selector = ((on_path[None, :] > 0.5) & (depth[None, :] == slot_ids[:, None] - length)).astype(
        jnp.float32
    )
    placed_keys = jnp.dot(selector, new_keys.astype(jnp.float32), precision=lax.Precision.HIGHEST)
    placed_values = jnp.dot(
        selector, new_values.astype(jnp.float32), precision=lax.Precision.HIGHEST
    )
    placed = jnp.stack([placed_keys, placed_values]).astype(jnp.bfloat16)
    written = jnp.sum(selector, axis=1) > 0.5
    logical = jnp.where(written[None, :, None], placed, logical)
    return jnp.transpose(
        logical.reshape(2, logical_pages.shape[0], logical_pages.shape[2], HD), (1, 0, 2, 3)
    )


def shards(
    tokens,
    query_weight,
    keyvalue_weight,
    output_weight,
    cache,
    page_table,
    parents,
    cache_len,
    accepted_leaf,
):
    head_count = lax.axis_size("head")
    head_index = lax.axis_index("head")
    tok_index = lax.axis_index("tok")
    requests = parents.shape[0]
    assert requests == head_count
    pages_dev = cache.shape[0]
    part_rows = query_weight.shape[0]
    q_cols = (HQ * HD) // head_count
    kv_cols = (2 * HD) // head_count
    out_cols = output_weight.shape[1]
    wq_piece = lax.dynamic_slice_in_dim(query_weight, head_index * q_cols, q_cols, axis=1)
    wkv_piece = lax.dynamic_slice_in_dim(keyvalue_weight, head_index * kv_cols, kv_cols, axis=1)
    flat = jnp.concatenate(
        [wq_piece.reshape(-1), wkv_piece.reshape(-1), output_weight.reshape(-1)]
    )
    stacked = lax.all_gather(flat, "tok", axis=0, tiled=False)
    tok_count = stacked.shape[0]
    n_q = part_rows * q_cols
    n_kv = part_rows * kv_cols
    wq_cols = stacked[:, :n_q].reshape(tok_count * part_rows, q_cols)
    wkv_cols = stacked[:, n_q : n_q + n_kv].reshape(tok_count * part_rows, kv_cols)
    wo_cols = (
        stacked[:, n_q + n_kv :]
        .reshape(tok_count, HQ * HD, out_cols)
        .transpose(1, 0, 2)
        .reshape(HQ * HD, tok_count * out_cols)
    )
    gathered = lax.all_gather(tokens, "head", axis=1, tiled=True)
    wide = gathered.astype(jnp.float32)
    mean_square = jnp.mean(wide * wide, axis=1, keepdims=True)
    normed = (wide * lax.rsqrt(mean_square + 1e-06)).astype(jnp.bfloat16)
    q_part = jnp.dot(normed, wq_cols, preferred_element_type=jnp.float32)
    kv_part = jnp.dot(normed, wkv_cols, preferred_element_type=jnp.float32)
    both = jnp.concatenate([q_part, kv_part], axis=1)
    mine = lax.all_to_all(both, "head", 0, 1, tiled=True)
    mine = mine.reshape(DRAFT, head_count, q_cols + kv_cols)
    q_pre = mine[:, :, :q_cols].reshape(DRAFT, HQ, HD)
    kv_pre = mine[:, :, q_cols:].reshape(DRAFT, 2 * HD)
    parent_row = lax.dynamic_index_in_dim(parents, head_index, 0, keepdims=False)
    length = lax.dynamic_index_in_dim(cache_len, head_index, 0, keepdims=False)
    leaf = lax.dynamic_index_in_dim(accepted_leaf, head_index, 0, keepdims=False)
    reach, depth = ancestry(parent_row)
    position = length + depth
    queries = (rotate(q_pre, position[:, None]) * HD ** (-0.5)).astype(jnp.bfloat16)
    tree_keys = rotate(kv_pre[:, :HD], position).astype(jnp.bfloat16)
    tree_values = kv_pre[:, HD:].astype(jnp.bfloat16)
    device = tok_index * head_count + head_index
    own_table = (
        lax.dynamic_index_in_dim(page_table, head_index, 0, keepdims=False) - device * pages_dev
    )
    own_pages = jnp.take(cache, own_table, axis=0)
    cache_keys = own_pages[:, 0].reshape(NPR * PAGE, HD)
    cache_values = own_pages[:, 1].reshape(NPR * PAGE, HD)
    result = attend(
        queries[None],
        cache_keys[None],
        cache_values[None],
        tree_keys[None],
        tree_values[None],
        length[None],
        position[None],
        reach[None],
    )
    mixed = lax.all_gather(result.reshape(DRAFT, HQ * HD), "head", axis=0, tiled=True)
    summed = jnp.zeros((mixed.shape[0], wo_cols.shape[1]), jnp.float32)
    for group in range(head_count):
        head_ids = [k for k in range(group, HQ, head_count)]
        if not head_ids:
            continue
        columns = jnp.concatenate([mixed[:, k * HD : (k + 1) * HD] for k in head_ids], axis=1)
        rows = jnp.concatenate([wo_cols[k * HD : (k + 1) * HD] for k in head_ids], axis=0)
        partial_value = jnp.dot(columns, rows, preferred_element_type=jnp.float32)
        summed = summed + partial_value.astype(jnp.bfloat16).astype(jnp.float32)
    attended = summed.astype(jnp.bfloat16)
    new_pages = refresh(own_pages, length, leaf, reach, depth, tree_keys, tree_values)
    matches = (own_table[:, None] == jnp.arange(pages_dev, dtype=jnp.int32)[None, :]).astype(
        jnp.int32
    )
    inverse = jnp.sum(matches * jnp.arange(pages_dev, dtype=jnp.int32)[:, None], axis=0)
    cache_out = jnp.take(new_pages, inverse, axis=0)
    return (attended, cache_out)


def solution(mesh):
    in_specs = (
        P("tok", "head"),
        P("tok", None),
        P("tok", None),
        P(None, ("head", "tok")),
        P(("tok", "head"), None, None, None),
        P("tok", None),
        P("tok", None),
        P("tok"),
        P("tok"),
    )
    out_specs = (P("tok", "head"), P(("tok", "head"), None, None, None))
    return jax.shard_map(shards, mesh=mesh, in_specs=in_specs, out_specs=out_specs, check_vma=False)
```

time: 583 us -> 287 us (0.49)
  waiting for transfers between devices: 481 us -> 186 us
  blocking collectives: 19.8 us -> 0 us
  local copies, waits for them, and re-layouts: 33.8 us -> 51.5 us
  starting transfers between devices: 0.24 us -> 12.8 us
  matrix products: 18.1 us -> 10.8 us
    all_gather x4 -> x2, waiting for transfers between devices: 430 us -> 146 us  [the longest x1 146 us: shards(): stacked = lax.all_gather(flat, 'tok', axis=0, tiled=False)]
    reduce_scatter x1 -> x0, waiting for transfers between devices: 37.3 us -> none  [reduce_heads(): lax.psum_scatter(partial_value.astype(jnp.float32).astype(jnp.bfloat16),...]
    slice x2 -> x30, local copies, waits for them, and re-layouts: 1.22 us -> 26 us  [the longest x21 19.2 us: shards(): wo_cols[k * HD:(k + 1) * HD]]
    all_gather x1 -> x0, blocking collectives: 19.8 us -> none  [reduce_heads(): blocks = lax.all_gather(output_weight, 'head', axis=1, tiled=True)]
    all_gather x1, waiting for transfers between devices: 11.9 us -> 29.1 us  [shards(): gathered = lax.all_gather(tokens, 'head', axis=1, tiled=True)]
    all_to_all x0 -> x1, starting transfers between devices: none -> 12.7 us  [shards(): mine = lax.all_to_all(both, 'head', 0, 1, tiled=True)]
    all_to_all x0 -> x1, waiting for transfers between devices: none -> 10 us  [shards(): mine = lax.all_to_all(both, 'head', 0, 1, tiled=True)]
    gather x7 -> x2, local copies, waits for them, and re-layouts: 7.34 us -> 1.16 us  [the longest x1 0.58 us: shards(): own_pages = jnp.take(cache, own_table, axis=0)]
  transfers between devices with their start and end apart: 6 -> 4, of which waited for: 6 -> 3; matrix products, arithmetic and copies ran while one was open for 7% -> 16% of each run, Pallas kernels for 0% -> 0%
where the time goes in v1:
time: 287 us; the launch traced here: 286 us
  waiting for transfers between devices  186 us (65%)
  local copies, waits for them, and re-layouts  51.5 us (18%)
  between operations  16.5 us (6%)
  starting transfers between devices  12.8 us (4%)
  matrix products  10.8 us (4%)
  other arithmetic  7.81 us (3%)
    all_gather x1, waiting for transfers between devices, shards(): stacked = lax.all_gather(flat, 'tok', axis=0, tiled=False)  146 us
    all_gather x1, waiting for transfers between devices, shards(): gathered = lax.all_gather(tokens, 'head', axis=1, tiled=True)  29.1 us
    slice x21, local copies, waits for them, and re-layouts, shards(): wo_cols[k * HD:(k + 1) * HD]  19.2 us
    all_to_all x1, starting transfers between devices, shards(): mine = lax.all_to_all(both, 'head', 0, 1, tiled=True)  12.7 us
    all_to_all x1, waiting for transfers between devices, shards(): mine = lax.all_to_all(both, 'head', 0, 1, tiled=True)  10 us
    reshape x1, local copies, waits for them, and re-layouts, shards(): wo_cols = stacked[:, n_q + n_kv:].reshape(tok_count, HQ * HD, out_cols).t...  7.08 us
    unnamed x29, local copies, waits for them, and re-layouts  6.45 us
  transfers between devices with their start and end apart: 4, of which 3 were waited for; matrix products, arithmetic and copies ran while one was open for 16% of the time, Pallas kernels for 0%

profile of v1, /device:TPU:1, one launch (start us, length us, event | category | flops | bytes accessed | tf_op | source)
XLA Modules:
  0.0 285.6 jit_solution(11939136876773440064)
XLA Ops:
  7.2 0.7 all-gather.6.cloned.1.call-update
  8.0 0.9 constant_dynamic-slice_fusion.2
  9.0 0.8 constant_dynamic-slice_fusion.1
  9.8 1.2 copy.62
  11.0 1.0 reshape.334
  12.0 0.7 reshape.362
  12.7 1.3 dynamic_slice.29
  15.4 1.2 dynamic_slice.25
  16.7 0.7 fusion.70
  19.5 0.7 iota_subtract_fusion
  20.4 29.1 %all-gather.6.cloned.1.call-done = bf16[512,2560]{0,1:T(8,128)(2,1)} async-done(((bf16[512,320]{0,1:T(8,128)(2,1)}), bf16[512,2560]{0,1:T(8,128)(2,1)}) %all-gather.6.cloned.1.call-update) | async-done | bytes 2621456 | tf_op jit(solution)/shard_map/all_gather | solution.py:129
  49.5 2.4 fusion
  51.9 146.4 %all-gather.10.cloned.1.call-done = bf16[64,1,28160]{2,1,0:T(2,128)(2,1)} async-done(((bf16[1,1,28160]{2,1,0:T(2,128)(2,1)}), bf16[64,1,28160]{2,1,0:T(2,128)(2,1)}) %all-gather.10.cloned.1.call-update) | async-done | bytes 3604496 | tf_op jit(solution)/shard_map/all_gather | solution.py:117
  198.3 3.5 %copy.97 = bf16[64,1,28160]{2,0,1:T(8,128)(2,1)S(1)} copy(bf16[64,1,28160]{2,1,0:T(2,128)(2,1)} %all-gather.10.cloned.1.call-done) | data formatting | bytes 7208960
  201.7 1.4 fusion.79
  203.1 2.5 reshape.335
  205.6 0.4 reshape.336
  206.0 3.6 %fusion.4 = f32[512,320]{0,1:T(8,128)S(1)} fusion(bf16[2560,320]{1,0:T(8,128)(2,1)} %reshape.335, bf16[512,2560]{0,1:T(8,128)(2,1)} %all-gather.6.cloned.1.call-done, f32[512]{0:T(512)S(1)} %add_rsqrt_fusion), kind=kOutput, calls=%fused_computation.8 | convolution fusion | flops 842792960 | bytes 4917248 | tf_op jit(solution)/shard_map/dot_general | solution.py:133
  209.7 0.7 fusion.2
  210.5 1.2 copy.63
  211.6 12.7 %all-to-all-start = ((f32[8,64,384]{2,1,0:T(8,128)}), f32[8,64,384]{2,1,0:T(8,128)S(1)}, u32[]{:S(2)}, u32[]{:S(2)}) async-start(f32[8,64,384]{2,1,0:T(8,128)} %bitcast.6), calls=%async_computation | async-start | bytes 1572864 | tf_op jit(solution)/shard_map/all_to_all | solution.py:136
  224.3 0.6 iota_compare_fusion.6
  225.1 0.6 gather_fusion
  225.7 0.7 add_add_fusion
  226.4 10.0 %all-to-all-done = f32[8,64,384]{2,1,0:T(8,128)S(1)} async-done(((f32[8,64,384]{2,1,0:T(8,128)}), f32[8,64,384]{2,1,0:T(8,128)S(1)}, u32[]{:S(2)}, u32[]{:S(2)}) %all-to-all-start) | async-done | bytes 786464 | tf_op jit(solution)/shard_map/all_to_all | solution.py:136
  236.9 0.3 convolution_convert_fusion.8
  237.3 0.5 copy.64
  237.7 0.4 reshape.337
  238.6 0.3 convolution_convert_fusion.9
  239.0 1.0 fusion.36
  240.3 0.4 fusion.84
  240.7 0.5 fusion.83
  241.3 0.4 fusion.26
  241.7 0.3 fusion.50
  242.0 0.4 fusion.85
  242.5 0.7 copy.90
  243.5 2.9 %copy.72 = bf16[64,12800]{0,1:T(8,128)(2,1)} copy(bf16[64,12800]{1,0:T(8,128)(2,1)S(1)} %copy-done.1) | data formatting | bytes 3276800 | tf_op jit(solution)/shard_map/slice | solution.py:124
  246.4 7.1 %reshape.342 = bf16[64,2560,5]{0,2,1:T(8,128)(2,1)} reshape(bf16[64,12800]{0,1:T(8,128)(2,1)} %copy.72) | data formatting | bytes 3276800 | tf_op jit(solution)/shard_map/reshape | solution.py:125
  253.5 4.9 %fusion.78 = (bf16[256,64,5]{1,2,0:T(8,128)(2,1)S(1)}, bf16[256,64,5]{1,2,0:T(8,128)(2,1)S(1)}, bf16[256,64,5]{1,2,0:T(8,128)(2,1)S(1)}, bf16[256,64,5]{1,2,0:T(...) fusion(bf16[2560,64,5]{1,2,0:T(8,128)(2,1)} %bitcast.112), kind=kLoop, calls=%fused_computation.143 | loop fusion | bytes 3276800 | tf_op jit(solution)/shard_map/slice | solution.py:172
  258.4 1.5 copy.73
  259.9 0.7 slice.155
  260.7 1.5 copy.74
  262.1 0.7 slice.157
  262.9 1.5 copy.75
  264.4 0.7 slice.161
  265.1 1.5 copy.76
  266.6 0.7 slice.163
  267.4 1.5 copy.77
  268.9 0.7 slice.166
  269.6 0.4 copy.78
  270.0 0.7 slice.169
  270.8 0.4 copy.79
  271.3 0.4 copy.80
  271.8 0.4 copy.81
  272.4 0.4 copy.82
  272.9 0.6 gather_fusion.1
  273.5 0.9 broadcast_select_fusion
  274.4 1.4 fusion.80
  275.9 0.4 fusion.23
  276.3 0.4 fusion.22
  277.2 0.3 fusion.16
  277.5 0.3 fusion.14
  277.8 0.3 fusion.12
  278.1 1.0 fusion.10
  (77 shorter events, 4.6 us)
Async XLA Ops:
  7.2 217.9 %copy-start = (bf16[4,2,128,256]{3,2,1,0:T(8,128)(2,1)S(1)}, bf16[4,2,128,256]{3,2,1,0:T(8,128)(2,1)}, u32[]{:S(2)}) copy-start(bf16[4,2,128,256]{3,2,1,0:T(8,128)(2,1)} %param.15) | copy-start | bytes 1572868
  7.2 12.1 %copy-start.11 = (s32[8,4]{0,1:T(4,128)S(1)}, s32[8,4]{0,1:T(4,128)}, u32[]{:S(2)}) copy-start(s32[8,4]{0,1:T(4,128)} %param.16) | copy-start | bytes 388
  7.2 42.3 %all-gather.6.cloned.1.call-start = ((), (), s32[]{:S(2)}) async-start(), calls=%async_computation.1 | async-start | bytes 2949120 | tf_op jit(solution)/shard_map/all_gather | solution.py:129
  7.9 190.3 %all-gather.10.cloned.1.call-start = ((), (), s32[]{:S(2)}) async-start(), calls=%async_computation.3 | async-start | bytes 7321600 | tf_op jit(solution)/shard_map/all_gather | solution.py:117
  206.0 3.7 %copy-start.2 = (bf16[512,2560]{0,1:T(8,128)(2,1)S(1)}, bf16[512,2560]{0,1:T(8,128)(2,1)}, u32[]{:S(2)}) copy-start(bf16[512,2560]{0,1:T(8,128)(2,1)} %all-gather.6.cloned.1.call-done) | copy-start | bytes 7864324
  211.6 24.9 %all-to-all-start = ((f32[8,64,384]{2,1,0:T(8,128)}), f32[8,64,384]{2,1,0:T(8,128)S(1)}, u32[]{:S(2)}, u32[]{:S(2)}) async-start(f32[8,64,384]{2,1,0:T(8,128)} %bitcast.6), calls=%async_computation | async-start | bytes 1572864 | tf_op jit(solution)/shard_map/all_to_all | solution.py:136
  224.3 50.1 %all-gather.8.cloned.1.call-start = ((), (), s32[]{:S(2)}) async-start(), calls=%async_computation.2 | async-start | bytes 2949120 | tf_op jit(solution)/shard_map/all_gather | solution.py:165
  242.0 1.5 copy-start.1
  270.0 2.9 %copy-start.4 = (bf16[4,2,128,256]{3,2,1,0:T(8,128)(2,1)S(1)}, bf16[4,2,128,256]{3,2,1,0:T(8,128)(2,1)}, u32[]{:S(2)}) copy-start(bf16[4,2,128,256]{3,2,1,0:T(8,128)(2,1)} %get-tuple-element.3) | copy-start | bytes 1572868
  272.3 3.5 %copy-start.9 = (bf16[256,320]{0,1:T(8,128)(2,1)S(1)}, bf16[256,320]{0,1:T(8,128)(2,1)}, u32[]{:S(2)}) copy-start(bf16[256,320]{0,1:T(8,128)(2,1)} %slice.155) | copy-start | bytes 491524
  272.4 3.5 %copy-start.10 = (bf16[256,320]{0,1:T(8,128)(2,1)S(1)}, bf16[256,320]{0,1:T(8,128)(2,1)}, u32[]{:S(2)}) copy-start(bf16[256,320]{0,1:T(8,128)(2,1)} %slice.157) | copy-start | bytes 491524
  273.5 2.8 copy-start.5
  273.5 2.8 copy-start.6
  274.4 2.2 copy-start.7
  274.4 2.2 copy-start.3
  275.9 1.1 copy-start.8
Sparse Core Ops, SparseCore 0:
  10.1 39.3 all-gather.5
  53.1 145.1 all-gather.9
  243.4 27.9 all-gather.7

commit v2 on v1

--- a/solution.py
+++ b/solution.py
@@ -114,8 +114,11 @@
     flat = jnp.concatenate(
         [wq_piece.reshape(-1), wkv_piece.reshape(-1), output_weight.reshape(-1)]
     )
-    stacked = lax.all_gather(flat, "tok", axis=0, tiled=False)
-    tok_count = stacked.shape[0]
+    tok_count = lax.axis_size("tok")
+    lanes = 128
+    tiles = flat.reshape(-1, lanes)
+    copies = jnp.broadcast_to(tiles[None], (tok_count,) + tiles.shape)
+    stacked = lax.all_to_all(copies, "tok", 0, 0, tiled=True).reshape(tok_count, -1)
     n_q = part_rows * q_cols
     n_kv = part_rows * kv_cols
     wq_cols = stacked[:, :n_q].reshape(tok_count * part_rows, q_cols)

time: 287 us -> 282 us (0.983)
  waiting for transfers between devices: 186 us -> 164 us
  starting transfers between devices: 12.8 us -> 30.4 us
    all_gather x1 -> x0, waiting for transfers between devices: 146 us -> none  [shards(): stacked = lax.all_gather(flat, 'tok', axis=0, tiled=False)]
    all_to_all x0 -> x1, waiting for transfers between devices: none -> 121 us  [shards(): lax.all_to_all(copies, 'tok', 0, 0, tiled=True).reshape(tok_count, -1)]
    all_to_all x0 -> x1, starting transfers between devices: none -> 19.5 us  [shards(): lax.all_to_all(copies, 'tok', 0, 0, tiled=True).reshape(tok_count, -1)]
    unnamed x29 -> x32, local copies, waits for them, and re-layouts: 6.45 us -> 5.74 us
  transfers between devices with their start and end apart: 4 -> 4, of which waited for: 3 -> 3; matrix products, arithmetic and copies ran while one was open for 16% -> 14% of each run, Pallas kernels for 0% -> 0%
where the time goes in v2:
time: 282 us; the launch traced here: 281 us
  waiting for transfers between devices  164 us (58%)
  local copies, waits for them, and re-layouts  51.4 us (18%)
  starting transfers between devices  30.4 us (11%)
  between operations  16.7 us (6%)
  matrix products  10.8 us (4%)
  other arithmetic  7.82 us (3%)
    all_to_all x1, waiting for transfers between devices, shards(): lax.all_to_all(copies, 'tok', 0, 0, tiled=True).reshape(tok_count, -1)  121 us
    all_gather x1, waiting for transfers between devices, shards(): gathered = lax.all_gather(tokens, 'head', axis=1, tiled=True)  31.3 us
    all_to_all x1, starting transfers between devices, shards(): lax.all_to_all(copies, 'tok', 0, 0, tiled=True).reshape(tok_count, -1)  19.5 us
    slice x21, local copies, waits for them, and re-layouts, shards(): wo_cols[k * HD:(k + 1) * HD]  18.9 us
    all_to_all x1, starting transfers between devices, shards(): mine = lax.all_to_all(both, 'head', 0, 1, tiled=True)  10.9 us
    all_to_all x1, waiting for transfers between devices, shards(): mine = lax.all_to_all(both, 'head', 0, 1, tiled=True)  10 us
    reshape x1, local copies, waits for them, and re-layouts, shards(): wo_cols = stacked[:, n_q + n_kv:].reshape(tok_count, HQ * HD, out_cols).t...  7.16 us
    unnamed x32, local copies, waits for them, and re-layouts  5.74 us
  transfers between devices with their start and end apart: 4, of which 3 were waited for; matrix products, arithmetic and copies ran while one was open for 14% of the time, Pallas kernels for 0%

profile of v2, /device:TPU:1, one launch (start us, length us, event | category | flops | bytes accessed | tf_op | source)
XLA Modules:
  0.0 280.7 jit_solution(7692784864150303648)
XLA Ops:
  7.2 0.9 constant_dynamic-slice_fusion.2
  8.2 0.8 constant_dynamic-slice_fusion.1
  9.1 1.2 copy.39
  10.2 1.0 reshape.338
  11.2 2.3 broadcast_in_dim.44
  13.5 19.5 %all-to-all-start = ((bf16[64,220,128]{2,1,0:T(8,128)(2,1)}), bf16[64,220,128]{2,1,0:T(8,128)(2,1)}, u32[]{:S(2)}, u32[]{:S(2)}) async-start(bf16[64,220,128]{2,1,0:T(8,128)(2,1)} %broadcast_in_dim.44), calls=%async_computation | async-start | bytes 7340032 | tf_op jit(solution)/shard_map/all_to_all | solution.py:121
  33.1 0.7 all-gather.3.cloned.1.call-update
  33.8 0.6 dynamic_slice.29
  35.6 0.6 dynamic_slice.25
  36.2 0.7 fusion.70
  39.0 0.7 iota_subtract_fusion
  39.9 31.3 %all-gather.3.cloned.1.call-done = bf16[512,2560]{0,1:T(8,128)(2,1)} async-done(((bf16[512,320]{0,1:T(8,128)(2,1)}), bf16[512,2560]{0,1:T(8,128)(2,1)}) %all-gather.3.cloned.1.call-update) | async-done | bytes 2621456 | tf_op jit(solution)/shard_map/all_gather | solution.py:132
  71.3 2.4 fusion
  73.6 121.5 %all-to-all-done = bf16[64,220,128]{2,1,0:T(8,128)(2,1)} async-done(((bf16[64,220,128]{2,1,0:T(8,128)(2,1)}), bf16[64,220,128]{2,1,0:T(8,128)(2,1)}, u32[]{:S(2)}, u32[]{:S(2)}) %all-to-all-start) | async-done | bytes 3604512 | tf_op jit(solution)/shard_map/all_to_all | solution.py:121
  195.1 3.4 %copy.74 = bf16[8,8,220,128]{3,1,2,0:T(8,128)(2,1)S(1)} copy(bf16[8,8,220,128]{3,2,1,0:T(8,128)(2,1)} %bitcast.36) | data formatting | bytes 7208960
  198.5 1.4 fusion.79
  199.9 2.5 reshape.340
  202.4 0.4 reshape.341
  202.8 3.6 %fusion.4 = f32[512,320]{0,1:T(8,128)S(1)} fusion(bf16[2560,320]{1,0:T(8,128)(2,1)} %reshape.340, bf16[512,2560]{0,1:T(8,128)(2,1)} %all-gather.3.cloned.1.call-done, f32[512]{0:T(512)S(1)} %add_rsqrt_fusion), kind=kOutput, calls=%fused_computation.8 | convolution fusion | flops 842792960 | bytes 4917248 | tf_op jit(solution)/shard_map/dot_general | solution.py:136
  206.5 0.7 fusion.2
  207.2 1.1 copy.40
  208.4 10.9 %all-to-all-start.1 = ((f32[8,64,384]{2,1,0:T(8,128)}), f32[8,64,384]{2,1,0:T(8,128)S(1)}, u32[]{:S(2)}, u32[]{:S(2)}) async-start(f32[8,64,384]{2,1,0:T(8,128)} %bitcast.7), calls=%async_computation.1 | async-start | bytes 1572864 | tf_op jit(solution)/shard_map/all_to_all | solution.py:139
  219.3 0.6 iota_compare_fusion.6
  220.0 0.6 gather_fusion
  220.6 0.7 add_add_fusion
  221.4 10.0 %all-to-all-done.1 = f32[8,64,384]{2,1,0:T(8,128)S(1)} async-done(((f32[8,64,384]{2,1,0:T(8,128)}), f32[8,64,384]{2,1,0:T(8,128)S(1)}, u32[]{:S(2)}, u32[]{:S(2)}) %all-to-all-start.1) | async-done | bytes 786464 | tf_op jit(solution)/shard_map/all_to_all | solution.py:139
  231.9 0.3 convolution_convert_fusion.8
  232.2 0.5 copy.41
  232.7 0.4 reshape.342
  233.6 0.3 convolution_convert_fusion.9
  233.9 1.0 fusion.36
  235.2 0.4 fusion.84
  235.6 0.5 fusion.83
  236.2 0.4 fusion.26
  236.7 0.3 fusion.50
  237.0 0.4 fusion.85
  237.4 0.7 copy.67
  238.4 2.9 %copy.49 = bf16[64,12800]{0,1:T(8,128)(2,1)} copy(bf16[64,12800]{1,0:T(8,128)(2,1)S(1)} %copy-done.1) | data formatting | bytes 3276800 | tf_op jit(solution)/shard_map/slice | solution.py:127
  241.4 7.2 %reshape.347 = bf16[64,2560,5]{0,2,1:T(8,128)(2,1)} reshape(bf16[64,12800]{0,1:T(8,128)(2,1)} %copy.49) | data formatting | bytes 3276800 | tf_op jit(solution)/shard_map/reshape | solution.py:128
  248.5 4.6 %fusion.78 = (bf16[256,64,5]{1,2,0:T(8,128)(2,1)S(1)}, bf16[256,64,5]{1,2,0:T(8,128)(2,1)S(1)}, bf16[256,64,5]{1,2,0:T(8,128)(2,1)S(1)}, bf16[256,64,5]{1,2,0:T(...) fusion(bf16[2560,64,5]{1,2,0:T(8,128)(2,1)} %bitcast.115), kind=kLoop, calls=%fused_computation.143 | loop fusion | bytes 3276800 | tf_op jit(solution)/shard_map/slice | solution.py:175
  253.1 1.5 copy.50
  254.6 0.7 slice.155
  255.3 1.5 copy.51
  256.8 0.7 slice.157
  257.6 1.5 copy.52
  259.1 0.8 slice.161
  259.8 1.5 copy.53
  261.3 0.7 slice.163
  262.1 1.5 copy.54
  263.5 0.7 slice.166
  264.3 0.4 copy.55
  264.7 0.7 slice.169
  265.5 0.4 copy.56
  266.0 0.4 copy.57
  266.5 0.4 copy.58
  267.1 0.4 copy.59
  267.6 0.6 gather_fusion.1
  268.2 0.9 broadcast_select_fusion
  269.1 1.4 fusion.80
  270.6 0.4 fusion.23
  271.0 0.4 fusion.22
  272.0 0.3 fusion.16
  272.2 0.3 fusion.14
  272.8 1.0 fusion.10
  (80 shorter events, 4.8 us)
Async XLA Ops:
  7.2 212.9 %copy-start = (bf16[4,2,128,256]{3,2,1,0:T(8,128)(2,1)S(1)}, bf16[4,2,128,256]{3,2,1,0:T(8,128)(2,1)}, u32[]{:S(2)}) copy-start(bf16[4,2,128,256]{3,2,1,0:T(8,128)(2,1)} %param.15) | copy-start | bytes 1572868
  13.5 20.2 %copy-start.12 = (s32[8]{0:T(128)S(1)}, s32[8]{0:T(128)}, u32[]{:S(2)}) copy-start(s32[8]{0:T(128)} %param.19) | copy-start | bytes 100
  13.5 22.1 %copy-start.13 = (s32[8]{0:T(128)S(1)}, s32[8]{0:T(128)}, u32[]{:S(2)}) copy-start(s32[8]{0:T(128)} %param.18) | copy-start | bytes 100
  13.5 25.3 %copy-start.11 = (s32[8,4]{0,1:T(4,128)S(1)}, s32[8,4]{0,1:T(4,128)}, u32[]{:S(2)}) copy-start(s32[8,4]{0,1:T(4,128)} %param.16) | copy-start | bytes 388
  13.5 181.5 %all-to-all-start = ((bf16[64,220,128]{2,1,0:T(8,128)(2,1)}), bf16[64,220,128]{2,1,0:T(8,128)(2,1)}, u32[]{:S(2)}, u32[]{:S(2)}) async-start(bf16[64,220,128]{2,1,0:T(8,128)(2,1)} %broadcast_in_dim.44), calls=%async_computation | async-start | bytes 7340032 | tf_op jit(solution)/shard_map/all_to_all | solution.py:121
  33.0 38.3 %all-gather.3.cloned.1.call-start = ((), (), s32[]{:S(2)}) async-start(), calls=%async_computation.2 | async-start | bytes 2949120 | tf_op jit(solution)/shard_map/all_gather | solution.py:132
  202.8 3.6 %copy-start.2 = (bf16[512,2560]{0,1:T(8,128)(2,1)S(1)}, bf16[512,2560]{0,1:T(8,128)(2,1)}, u32[]{:S(2)}) copy-start(bf16[512,2560]{0,1:T(8,128)(2,1)} %all-gather.3.cloned.1.call-done) | copy-start | bytes 7864324
  208.4 23.0 %all-to-all-start.1 = ((f32[8,64,384]{2,1,0:T(8,128)}), f32[8,64,384]{2,1,0:T(8,128)S(1)}, u32[]{:S(2)}, u32[]{:S(2)}) async-start(f32[8,64,384]{2,1,0:T(8,128)} %bitcast.7), calls=%async_computation.1 | async-start | bytes 1572864 | tf_op jit(solution)/shard_map/all_to_all | solution.py:139
  219.3 49.9 %all-gather.5.cloned.1.call-start = ((), (), s32[]{:S(2)}) async-start(), calls=%async_computation.3 | async-start | bytes 2949120 | tf_op jit(solution)/shard_map/all_gather | solution.py:168
  237.0 1.5 copy-start.1
  264.7 2.9 %copy-start.4 = (bf16[4,2,128,256]{3,2,1,0:T(8,128)(2,1)S(1)}, bf16[4,2,128,256]{3,2,1,0:T(8,128)(2,1)}, u32[]{:S(2)}) copy-start(bf16[4,2,128,256]{3,2,1,0:T(8,128)(2,1)} %get-tuple-element.3) | copy-start | bytes 1572868
  267.1 3.5 %copy-start.9 = (bf16[256,320]{0,1:T(8,128)(2,1)S(1)}, bf16[256,320]{0,1:T(8,128)(2,1)}, u32[]{:S(2)}) copy-start(bf16[256,320]{0,1:T(8,128)(2,1)} %slice.155) | copy-start | bytes 491524
  267.1 3.5 %copy-start.10 = (bf16[256,320]{0,1:T(8,128)(2,1)S(1)}, bf16[256,320]{0,1:T(8,128)(2,1)}, u32[]{:S(2)}) copy-start(bf16[256,320]{0,1:T(8,128)(2,1)} %slice.157) | copy-start | bytes 491524
  268.2 2.8 copy-start.5
  268.2 2.8 copy-start.6
  269.1 2.2 copy-start.7
  269.1 2.2 copy-start.3
  270.6 1.1 copy-start.8
Sparse Core Ops, SparseCore 0:
  35.9 35.2 all-gather.2
  238.3 24.0 all-gather.4
